TPU v7x, 512 devices: a whole 4x8x8 slice. The times are simulated.
512 devices in a mesh: pp: 4 (over x_lo, core), cp: 16 (over z, x_hi), tp: 8 (over y).
Axes of the slice: x: 4 (x_hi: 2, x_lo: 2; x = x_hi * 2 + x_lo), y: 8, z: 8, core: 2. Of those that a mesh axis runs over, the one named last changes fastest.
Arguments:
- query: bfloat16 [4, 2048, 16384], P('pp', 'cp', 'tp'), may hold values from -200 to 200
- key: bfloat16 [4, 2048, 1024], P('pp', 'cp', 'tp'), may hold values from -6 to 6
- value: bfloat16 [4, 2048, 1024], P('pp', 'cp', 'tp'), may hold values from -6 to 6
- out_grad: bfloat16 [4, 2048, 16384], P('pp', 'cp', 'tp'), may hold values from -24 to 24
- lengths: int32 [6], replicated, may hold values from 1 to 1024, 2048 in all
- plan: int32 [16, 16], replicated, may hold values from 0 to 15, each once within a row
Outputs:
- handed_grad: bfloat16 [4, 2048, 16384], P('pp', 'cp', 'tp')
- key_grad: bfloat16 [4, 2048, 1024], P('pp', 'cp', 'tp')
- value_grad: bfloat16 [4, 2048, 1024], P('pp', 'cp', 'tp')
Inputs may be any that keep to these rules, and one draw needn't show every extreme that they name: Row s of plan is a permutation: for each of the blocks of 8 tokens of context shard s it names the shard that takes the block.
All inputs are finite; a program needn't handle non-finite values.
Results may differ from a plain program's by a relative error of at most 0.0085.
Values may be sent and summed in bfloat16 or wider, within the bound.
No kernel may reach another device: no remote copies, remote signals or barrier semaphores. Data moves between devices by JAX's collectives and lax.ppermute only.
A program may use at most 64 MiB of HBM per device.

v0:
```python
import jax
import jax.numpy as jnp
from jax import lax
from jax.sharding import PartitionSpec as P


def passed_along(array, axis, by):
    peers = lax.axis_size(axis)
    pairs = [(i, i + by) for i in range(peers) if 0 <= i + by < peers]
    return lax.ppermute(array, axis, pairs)


def attend(query_rows, grad_rows, query_pos, key_full, value_full, owner):
    tokens = query_rows.shape[0]
    head_width = key_full.shape[1]
    head_count = query_rows.shape[1] // head_width
    key_count = key_full.shape[0]
    total_rows = tokens * head_count
    score_scale = head_width ** (-0.5)
    flat_query = query_rows.reshape(total_rows, head_width)
    flat_grad = grad_rows.reshape(total_rows, head_width)
    row_pos = jnp.repeat(query_pos, head_count)
    row_doc = jnp.repeat(jnp.take(owner, query_pos), head_count)
    block_width = min(512, key_count)
    block_count = key_count // block_width
    key_pos = jnp.arange(key_count, dtype=jnp.int32)
    blocks = (
        key_full.reshape(block_count, block_width, head_width),
        value_full.reshape(block_count, block_width, head_width),
        key_pos.reshape(block_count, block_width),
        owner.reshape(block_count, block_width),
    )

    def masked_scores(key_block, pos_block, doc_block):
        scores = jnp.dot(flat_query, key_block.T, preferred_element_type=jnp.float32) * score_scale
        seen = (doc_block[None, :] == row_doc[:, None]) & (pos_block[None, :] <= row_pos[:, None])
        return jnp.where(seen, scores, -jnp.inf)

    def first_pass(state, block):
        top, total, weighted = state
        key_block, value_block, pos_block, doc_block = block
        scores = masked_scores(key_block, pos_block, doc_block)
        new_top = jnp.maximum(top, jnp.max(scores, axis=1))
        expo = jnp.exp(scores - new_top[:, None])
        shrink = jnp.exp(top - new_top)
        dprob = jnp.dot(flat_grad, value_block.T, preferred_element_type=jnp.float32)
        total = total * shrink + jnp.sum(expo, axis=1)
        weighted = weighted * shrink + jnp.sum(expo * dprob, axis=1)
        return ((new_top, total, weighted), None)

    start = (
        jnp.full((total_rows,), -1e30, jnp.float32),
        jnp.zeros((total_rows,), jnp.float32),
        jnp.zeros((total_rows,), jnp.float32),
    )
    (top, total, weighted), unused = lax.scan(first_pass, start, blocks)
    delta = weighted / total

    def second_pass(dquery, block):
        key_block, value_block, pos_block, doc_block = block
        scores = masked_scores(key_block, pos_block, doc_block)
        probs = jnp.exp(scores - top[:, None]) / total[:, None]
        dprob = jnp.dot(flat_grad, value_block.T, preferred_element_type=jnp.float32)
        probs_low = probs.astype(jnp.bfloat16)
        dscore = (probs * (dprob - delta[:, None]) * score_scale).astype(jnp.bfloat16)
        dvalue = jnp.dot(probs_low.T, flat_grad, preferred_element_type=jnp.float32)
        dkey = jnp.dot(dscore.T, flat_query, preferred_element_type=jnp.float32)
        dquery = dquery + jnp.dot(dscore, key_block, preferred_element_type=jnp.float32)
        return (dquery, jnp.concatenate([dkey, dvalue], axis=1))

    dquery, terms = lax.scan(second_pass, jnp.zeros((total_rows, head_width), jnp.float32), blocks)
    dquery = dquery.astype(jnp.bfloat16).reshape(tokens, head_count * head_width)
    return (dquery, terms.reshape(key_count, 2 * head_width))


def body(query, key, value, out_grad, lengths, plan):
    tokens = query.shape[1]
    width = query.shape[2]
    head_width = key.shape[2]
    shards = lax.axis_size("cp")
    own_index = lax.axis_index("cp")
    block_rows = tokens // shards
    key_full, value_full = (
        lax.all_gather(key[0], "cp", axis=0, tiled=True),
        lax.all_gather(value[0], "cp", axis=0, tiled=True),
    )
    key_count = key_full.shape[0]
    ends = jnp.cumsum(lengths)
    positions = jnp.arange(key_count, dtype=jnp.int32)
    owner = jnp.sum((positions[:, None] >= ends[None, :]).astype(jnp.int32), axis=1)
    iota = jnp.arange(shards, dtype=jnp.int32)
    inverse = jnp.sum(
        (plan[:, None, :] == iota[None, :, None]).astype(jnp.int32) * iota[None, None, :], axis=2
    )
    send_order = lax.dynamic_index_in_dim(inverse, own_index, 0, keepdims=False)

    def reorder(rows):
        grouped = rows.reshape(shards, block_rows, rows.shape[1])
        return jnp.take(grouped, send_order, axis=0)

    query_sent, grad_sent = (
        lax.all_to_all(reorder(query[0]), "cp", split_axis=0, concat_axis=0, tiled=True),
        lax.all_to_all(reorder(out_grad[0]), "cp", split_axis=0, concat_axis=0, tiled=True),
    )
    taken = lax.dynamic_index_in_dim(inverse, own_index, 1, keepdims=False)
    query_pos = (
        iota[:, None] * tokens
        + taken[:, None] * block_rows
        + jnp.arange(block_rows, dtype=jnp.int32)[None, :]
    ).reshape(tokens)
    dquery, terms = attend(
        query_sent.reshape(tokens, width),
        grad_sent.reshape(tokens, width),
        query_pos,
        key_full,
        value_full,
        owner,
    )
    handed = passed_along(dquery, "pp", -1)
    summed = lax.psum_scatter(terms, "cp", scatter_dimension=0, tiled=True)
    key_grad = summed[:, :head_width].astype(jnp.bfloat16)
    value_grad = summed[:, head_width:].astype(jnp.bfloat16)
    return (handed[None], key_grad[None], value_grad[None])


def solution(mesh):
    return jax.shard_map(
        body,
        mesh=mesh,
        in_specs=(
            P("pp", "cp", "tp"),
            P("pp", "cp", "tp"),
            P("pp", "cp", "tp"),
            P("pp", "cp", "tp"),
            P(),
            P(),
        ),
        out_specs=(P("pp", "cp", "tp"), P("pp", "cp", "tp"), P("pp", "cp", "tp")),
        check_vma=False,
    )
```

profile of v0, /device:TPU:8, one launch (start us, length us, event | category | flops | bytes accessed | tf_op | source)
XLA Modules:
  0.0 425.7 jit_solution(5239354460927206662)
XLA Ops:
  11.7 12.9 %all-to-all-start.1 = ((bf16[16,8,2048]{2,1,0:T(8,128)(2,1)}), bf16[16,8,2048]{2,1,0:T(8,128)(2,1)S(1)}, u32[]{:S(2)}, u32[]{:S(2)}) async-start(bf16[16,8,2048]{2,1,0:T(8,128)(2,1)} %get-tuple-element.306), calls=%async_computation.1 | async-start | bytes 1048576 | tf_op jit(solution)/shard_map/all_to_all | solution.py:103
  25.1 18.1 %all-to-all-done.1 = bf16[16,8,2048]{2,1,0:T(8,128)(2,1)S(1)} async-done(((bf16[16,8,2048]{2,1,0:T(8,128)(2,1)}), bf16[16,8,2048]{2,1,0:T(8,128)(2,1)S(1)}, u32[]{:S(2)}, u32[]{:S(2)}) %all-to-all-start.1) | async-done | bytes 524320 | tf_op jit(solution)/shard_map/all_to_all | solution.py:103
  43.2 3.6 all-to-all-start
  48.3 49.1 %all-gather = bf16[1,2048,128]{2,1,0:T(8,128)(2,1)} all-gather(bf16[1,128,128]{2,1,0:T(8,128)(2,1)S(1)} %copy-done.1), channel_id=2, replica_groups=mesh['pp'=4,'cp'=16,'tp'=8] {'cp'}, dimensions={1}, use_global_device_ids=true | all-gather | bytes 557056 | tf_op jit(solution)/shard_map/all_gather | solution.py:84
  97.4 43.7 %all-gather.1 = bf16[1,2048,128]{2,1,0:T(8,128)(2,1)} all-gather(bf16[1,128,128]{2,1,0:T(8,128)(2,1)S(1)} %copy-done.2), channel_id=3, replica_groups=mesh['pp'=4,'cp'=16,'tp'=8] {'cp'}, dimensions={1}, use_global_device_ids=true | all-gather | bytes 557056 | tf_op jit(solution)/shard_map/all_gather | solution.py:85
  142.4 20.0 %while.28 = (s32[]{:T(128)}, f32[2048]{0:T(1024)S(1)}, f32[2048]{0:T(1024)S(1)}, f32[2048]{0:T(1024)S(1)}, s32[4,512]{1,0:T(4,128)S(1)}, /*index=5*/s32[4,512]{1...) while((s32[]{:T(128)}, f32[2048]{0:T(1024)S(1)}, ...), condition=%wide.region_7.9_spmd.clone, body=%wide.region_3.0_spmd.clone.sunk | while | flops 548419584 | bytes 14120100 | solution.py:56
  142.8 2.2 fusion.69
  145.0 1.8 fusion.70
  147.8 2.2 fusion.69
  150.0 1.8 fusion.70
  152.8 2.2 fusion.69
  155.0 1.8 fusion.70
  157.8 2.2 fusion.69
  160.0 1.8 fusion.70
  162.5 41.5 %while.29 = (s32[]{:T(128)}, f32[2048,128]{1,0:T(8,128)S(1)}, f32[4,512,256]{2,1,0:T(8,128)}, s32[4,512]{1,0:T(4,128)S(1)}, s32[4,512]{1,0:T(4,128)S(1)}, /*inde...) while((s32[]{:T(128)}, f32[2048,128]{1,0:T(8,128)S(1)}, ...), condition=%wide.region_9.11_spmd.clone, body=%wide.region_8.10_spmd.clone.sunk | while | flops 1355415552 | bytes 27235516 | solution.py:71
  162.8 2.6 fusion.83
  166.3 1.6 fusion.84
  167.9 1.9 fusion.86
  169.8 2.0 convolution_add_fusion.2
  173.2 2.6 fusion.83
  176.6 1.6 fusion.84
  178.3 1.9 fusion.86
  180.2 2.0 convolution_add_fusion.2
  183.6 2.6 fusion.83
  188.7 1.9 fusion.86
  190.5 2.0 convolution_add_fusion.2
  194.0 2.6 fusion.83
  197.4 1.6 fusion.84
  199.1 1.9 fusion.86
  200.9 2.0 convolution_add_fusion.2
  205.6 2.5 collective-permute-done
  208.1 208.4 %reduce-scatter.2.cloned.1.call-done = f32[128,256]{1,0:T(8,128)} async-done(((f32[2048,256]{1,0:T(8,128)}), f32[128,256]{1,0:T(8,128)}) %reduce-scatter.2.cloned.1.call-update) | async-done | bytes 131088 | tf_op jit(solution)/shard_map/reduce_scatter | solution.py:120
  (116 shorter events, 26.3 us)
Async XLA Ops:
  7.2 1.2 copy-start
  7.2 17.4 %copy-start.3 = (s32[6]{0:T(128)S(1)}, s32[6]{0:T(128)}, u32[]{:S(2)}) copy-start(s32[6]{0:T(128)} %param.16) | copy-start | bytes 76
  7.2 41.1 %copy-start.1 = (bf16[1,128,128]{2,1,0:T(8,128)(2,1)S(1)}, bf16[1,128,128]{2,1,0:T(8,128)(2,1)}, u32[]{:S(2)}) copy-start(bf16[1,128,128]{2,1,0:T(8,128)(2,1)} %param.13) | copy-start | bytes 98308
  7.2 90.2 %copy-start.2 = (bf16[1,128,128]{2,1,0:T(8,128)(2,1)S(1)}, bf16[1,128,128]{2,1,0:T(8,128)(2,1)}, u32[]{:S(2)}) copy-start(bf16[1,128,128]{2,1,0:T(8,128)(2,1)} %param.14) | copy-start | bytes 98308
  11.7 31.5 %all-to-all-start.1 = ((bf16[16,8,2048]{2,1,0:T(8,128)(2,1)}), bf16[16,8,2048]{2,1,0:T(8,128)(2,1)S(1)}, u32[]{:S(2)}, u32[]{:S(2)}) async-start(bf16[16,8,2048]{2,1,0:T(8,128)(2,1)} %get-tuple-element.306), calls=%async_computation.1 | async-start | bytes 1048576 | tf_op jit(solution)/shard_map/all_to_all | solution.py:103
  43.2 98.1 %all-to-all-start = ((bf16[16,8,2048]{2,1,0:T(8,128)(2,1)}), bf16[16,8,2048]{2,1,0:T(8,128)(2,1)S(1)}, u32[]{:S(2)}, u32[]{:S(2)}) async-start(bf16[16,8,2048]{2,1,0:T(8,128)(2,1)} %get-tuple-element.307), calls=%async_computation | async-start | bytes 1048576 | tf_op jit(solution)/shard_map/all_to_all | solution.py:102
  46.8 369.7 %reduce-scatter.2.cloned.1.call-start = ((), (), s32[]{:S(2)}) async-start(), calls=%async_computation.3 | async-start | bytes 2228224 | tf_op jit(solution)/shard_map/reduce_scatter | solution.py:120
  204.3 3.8 collective-permute-start
Sparse Core Ops, SparseCore 0:
  204.1 212.3 reduce-scatter.1
where the time goes:
time: 427 us; the launch traced here: 426 us
  waiting for transfers between devices  229 us (54%)
  blocking collectives  92.8 us (22%)
  matrix products  51.4 us (12%)
  starting transfers between devices  17.8 us (4%)
  between operations  14.3 us (3%)
  local copies, waits for them, and re-layouts  13.4 us (3%)
  other arithmetic  6.55 us (2%)
    reduce_scatter x1, waiting for transfers between devices, body(): summed = lax.psum_scatter(terms, 'cp', scatter_dimension=0, tiled=True)  208 us
    all_gather x1, blocking collectives, body(): lax.all_gather(key[0], 'cp', axis=0, tiled=True)  49.1 us
    all_gather x1, blocking collectives, body(): lax.all_gather(value[0], 'cp', axis=0, tiled=True)  43.7 us
    dot_general x8, matrix products, masked_scores(): jnp.dot(flat_query, key_block.T, preferred_element_type=jnp.float32)  19 us
    all_to_all x1, waiting for transfers between devices, body(): lax.all_to_all(reorder(out_grad[0]), 'cp', split_axis=0, concat_axis=0, t...  18.1 us
    all_to_all x1, starting transfers between devices, body(): lax.all_to_all(reorder(out_grad[0]), 'cp', split_axis=0, concat_axis=0, t...  12.9 us
  transfers between devices with their start and end apart: 4, of which 3 were waited for; matrix products, arithmetic and copies ran while one was open for 1% of the time, Pallas kernels for 0%

commit v1 on v0

--- a/solution.py
+++ b/solution.py
@@ -81,7 +81,9 @@
     own_index = lax.axis_index("cp")
     block_rows = tokens // shards
     key_full, value_full = (
-        lax.all_gather(key[0], "cp", axis=0, tiled=True),
+        jnp.concatenate(
+            lax.all_to_all(jnp.stack([key[0]] * lax.axis_size("cp"), axis=0), "cp", 0, 0), 0
+        ),
         lax.all_gather(value[0], "cp", axis=0, tiled=True),
     )
     key_count = key_full.shape[0]

time: 427 us -> 406 us (0.951)
  blocking collectives: 92.8 us -> 79.8 us
  starting transfers between devices: 17.8 us -> 9.14 us
    all_gather x1 -> x0, blocking collectives: 49.1 us -> none  [body(): lax.all_gather(key[0], 'cp', axis=0, tiled=True)]
    all_to_all x0 -> x1, blocking collectives: none -> 31.3 us  [body(): lax.all_to_all(reorder(out_grad[0]), 'cp', split_axis=0, concat_axis=0, t...]
    all_to_all x1, waiting for transfers between devices: 18.1 us -> 0.01 us  [body(): lax.all_to_all(jnp.stack([key[0]] * lax.axis_size('cp'), axis=0), 'cp', 0...]
    all_to_all x1, waiting for transfers between devices: 0.01 us -> 17.7 us  [body(): lax.all_to_all(reorder(query[0]), 'cp', split_axis=0, concat_axis=0, tile...]
    all_to_all x1, starting transfers between devices: 12.9 us -> 4.24 us  [body(): lax.all_to_all(jnp.stack([key[0]] * lax.axis_size('cp'), axis=0), 'cp', 0...]
    all_gather x1, blocking collectives: 43.7 us -> 48.4 us  [body(): lax.all_gather(value[0], 'cp', axis=0, tiled=True)]
where the time goes in v1:
time: 406 us; the launch traced here: 405 us
  waiting for transfers between devices  229 us (56%)
  blocking collectives  79.8 us (20%)
  matrix products  51.4 us (13%)
  local copies, waits for them, and re-layouts  14.3 us (4%)
  between operations  14.3 us (4%)
  starting transfers between devices  9.14 us (2%)
  other arithmetic  6.39 us (2%)
    reduce_scatter x1, waiting for transfers between devices, body(): summed = lax.psum_scatter(terms, 'cp', scatter_dimension=0, tiled=True)  209 us
    all_gather x1, blocking collectives, body(): lax.all_gather(value[0], 'cp', axis=0, tiled=True)  48.4 us
    all_to_all x1, blocking collectives, body(): lax.all_to_all(reorder(out_grad[0]), 'cp', split_axis=0, concat_axis=0, t...  31.3 us
    dot_general x8, matrix products, masked_scores(): jnp.dot(flat_query, key_block.T, preferred_element_type=jnp.float32)  19 us
    all_to_all x1, waiting for transfers between devices, body(): lax.all_to_all(reorder(query[0]), 'cp', split_axis=0, concat_axis=0, tile...  17.7 us
  transfers between devices with their start and end apart: 4, of which 3 were waited for; matrix products, arithmetic and copies ran while one was open for 1% of the time, Pallas kernels for 0%

profile of v1, /device:TPU:8, one launch (start us, length us, event | category | flops | bytes accessed | tf_op | source)
XLA Modules:
  0.0 404.7 jit_solution(10056897531075750914)
XLA Ops:
  11.5 31.3 %all_to_all.15 = bf16[16,8,2048]{2,1,0:T(8,128)(2,1)S(1)} all-to-all(bf16[16,8,2048]{2,1,0:T(8,128)(2,1)S(1)} %get-tuple-element.306), channel_id=1, replica_groups=mesh['pp'=4,'cp'=16,'tp'=8] {'cp'}, dimensions={0} | all-to-all | bytes 1048576 | tf_op jit(solution)/shard_map/all_to_all | solution.py:105
  42.9 3.6 all-to-all-start.1
  47.1 17.7 %all-to-all-done.1 = bf16[16,8,2048]{2,1,0:T(8,128)(2,1)S(1)} async-done(((bf16[16,8,2048]{2,1,0:T(8,128)(2,1)}), bf16[16,8,2048]{2,1,0:T(8,128)(2,1)S(1)}, u32[]{:S(2)}, u32[]{:S(2)}) %all-to-all-start.1) | async-done | bytes 524320 | tf_op jit(solution)/shard_map/all_to_all | solution.py:104
  65.7 4.2 %all-to-all-start = ((bf16[16,128,128]{2,1,0:T(8,128)(2,1)}), bf16[16,128,128]{2,1,0:T(8,128)(2,1)}, u32[]{:S(2)}, u32[]{:S(2)}) async-start(bf16[16,128,128]{2,1,0:T(8,128)(2,1)} %stack.3), calls=%async_computation | async-start | bytes 1048576 | tf_op jit(solution)/shard_map/all_to_all | solution.py:85
  71.3 48.4 %all-gather = bf16[1,2048,128]{2,1,0:T(8,128)(2,1)} all-gather(bf16[1,128,128]{2,1,0:T(8,128)(2,1)S(1)} %copy-done.2), channel_id=2, replica_groups=mesh['pp'=4,'cp'=16,'tp'=8] {'cp'}, dimensions={1}, use_global_device_ids=true | all-gather | bytes 557056 | tf_op jit(solution)/shard_map/all_gather | solution.py:87
  121.1 20.0 %while.28 = (s32[]{:T(128)}, f32[2048]{0:T(1024)S(1)}, f32[2048]{0:T(1024)S(1)}, f32[2048]{0:T(1024)S(1)}, s32[4,512]{1,0:T(4,128)S(1)}, /*index=5*/s32[4,512]{1...) while((s32[]{:T(128)}, f32[2048]{0:T(1024)S(1)}, ...), condition=%wide.region_7.9_spmd.clone, body=%wide.region_3.0_spmd.clone.sunk | while | flops 548419584 | bytes 14120100 | solution.py:56
  121.4 2.2 fusion.69
  123.6 1.8 fusion.70
  126.4 2.2 fusion.69
  128.6 1.8 fusion.70
  131.5 2.2 fusion.69
  133.7 1.8 fusion.70
  136.5 2.2 fusion.69
  138.7 1.8 fusion.70
  141.2 41.5 %while.29 = (s32[]{:T(128)}, f32[2048,128]{1,0:T(8,128)S(1)}, f32[4,512,256]{2,1,0:T(8,128)}, s32[4,512]{1,0:T(4,128)S(1)}, s32[4,512]{1,0:T(4,128)S(1)}, /*inde...) while((s32[]{:T(128)}, f32[2048,128]{1,0:T(8,128)S(1)}, ...), condition=%wide.region_9.11_spmd.clone, body=%wide.region_8.10_spmd.clone.sunk | while | flops 1355415552 | bytes 27235516 | solution.py:71
  141.5 2.6 fusion.83
  145.0 1.6 fusion.84
  146.6 1.9 fusion.86
  148.5 2.0 convolution_add_fusion.2
  151.9 2.6 fusion.83
  155.3 1.6 fusion.84
  156.9 1.9 fusion.86
  158.8 2.0 convolution_add_fusion.2
  162.2 2.6 fusion.83
  165.7 1.6 fusion.84
  167.3 1.9 fusion.86
  169.2 2.0 convolution_add_fusion.2
  172.6 2.6 fusion.83
  177.7 1.9 fusion.86
  179.6 2.0 convolution_add_fusion.2
  184.3 2.5 collective-permute-done
  186.8 208.8 %reduce-scatter.2.cloned.1.call-done = f32[128,256]{1,0:T(8,128)} async-done(((f32[2048,256]{1,0:T(8,128)}), f32[128,256]{1,0:T(8,128)}) %reduce-scatter.2.cloned.1.call-update) | async-done | bytes 131088 | tf_op jit(solution)/shard_map/reduce_scatter | solution.py:122
  (117 shorter events, 27.0 us)
Async XLA Ops:
  7.2 1.2 copy-start
  7.2 39.8 %copy-start.3 = (s32[6]{0:T(128)S(1)}, s32[6]{0:T(128)}, u32[]{:S(2)}) copy-start(s32[6]{0:T(128)} %param.16) | copy-start | bytes 76
  7.2 57.6 %copy-start.1 = (bf16[1,128,128]{2,1,0:T(8,128)(2,1)S(1)}, bf16[1,128,128]{2,1,0:T(8,128)(2,1)}, u32[]{:S(2)}) copy-start(bf16[1,128,128]{2,1,0:T(8,128)(2,1)} %param.13) | copy-start | bytes 98308
  8.3 63.0 %copy-start.2 = (bf16[1,128,128]{2,1,0:T(8,128)(2,1)S(1)}, bf16[1,128,128]{2,1,0:T(8,128)(2,1)}, u32[]{:S(2)}) copy-start(bf16[1,128,128]{2,1,0:T(8,128)(2,1)} %param.14) | copy-start | bytes 98308
  42.9 22.0 %all-to-all-start.1 = ((bf16[16,8,2048]{2,1,0:T(8,128)(2,1)}), bf16[16,8,2048]{2,1,0:T(8,128)(2,1)S(1)}, u32[]{:S(2)}, u32[]{:S(2)}) async-start(bf16[16,8,2048]{2,1,0:T(8,128)(2,1)} %get-tuple-element.307), calls=%async_computation.1 | async-start | bytes 1048576 | tf_op jit(solution)/shard_map/all_to_all | solution.py:104
  65.7 55.4 %all-to-all-start = ((bf16[16,128,128]{2,1,0:T(8,128)(2,1)}), bf16[16,128,128]{2,1,0:T(8,128)(2,1)}, u32[]{:S(2)}, u32[]{:S(2)}) async-start(bf16[16,128,128]{2,1,0:T(8,128)(2,1)} %stack.3), calls=%async_computation | async-start | bytes 1048576 | tf_op jit(solution)/shard_map/all_to_all | solution.py:85
  70.0 325.6 %reduce-scatter.2.cloned.1.call-start = ((), (), s32[]{:S(2)}) async-start(), calls=%async_computation.4 | async-start | bytes 2228224 | tf_op jit(solution)/shard_map/reduce_scatter | solution.py:122
  183.0 3.8 collective-permute-start
Sparse Core Ops, SparseCore 0:
  182.8 212.7 reduce-scatter.1
